TPU v7x, 32 devices: a whole 2x2x4 slice. The times are simulated.
32 devices in a mesh: group: 2 (over y), sub: 4 (over z), tile: 2 (over x), rep: 2 (over core).
Axes of the slice: x: 2, y: 2, z: 4, core: 2. Of those that a mesh axis runs over, the one named last changes fastest.
Arguments:
- right_side: bfloat16 [16, 1024, 512], P(('group', 'sub', 'tile'), None, 'rep'), parts along dimension 0, may hold values from -6 to 6
- interface_inverse: bfloat16 [16, 1024, 1024], P(('group', 'sub', 'tile')), parts along dimension 0, may hold values from -0.1875 to 0.1875
- coupling: float32 [16, 2, 128], P(('group', 'sub', 'tile')), parts along dimension 0, may hold values from 0.5 to 2
- trace_rows: int32 [16, 2, 128], P(('group', 'sub', 'tile')), parts along dimension 0, may hold values from 0 to 1023
- deflation_basis: bfloat16 [16, 1024, 128], P(('group', 'sub', 'tile')), parts along dimension 0, may hold values from -0.375 to 0.375
- deflation_counts: int32 [16], P(('group', 'sub', 'tile')), parts along dimension 0, may hold values from 32 to 128, as said below
- coarse_inverse: bfloat16 [8, 2, 128, 4, 256], P('group', 'tile', 'rep', 'sub'), parts along dimension 0, may hold values from -0.25 to 0.25
Outputs:
- corrected_field: bfloat16 [16, 1024, 512], P(('group', 'sub', 'tile'), None, 'rep'), parts along dimension 0
There are 2 independent parts, one for each index of `group`. A program takes and returns all parts, laid end to end along the dimension named above; each array names one. Nothing has to cross between parts.
Inputs may be any that keep to these rules, and one draw needn't show every extreme that they name: `deflation_counts`: some subdomain has exactly 128 live deflation vectors.
All inputs are finite; a program needn't handle non-finite values.
Results may differ from a plain program's by a relative error of at most 0.035.
Values may be sent and summed in bfloat16 or wider, within the bound.
No kernel may reach another device: no remote copies, remote signals or barrier semaphores. Data moves between devices by JAX's collectives and lax.ppermute only.
A program may use at most 64 MiB of HBM per device.

v0:
```python
import jax
import jax.numpy as jnp
from jax import lax
from jax.sharding import PartitionSpec as P

ROUNDS = 2
DUCT = ("sub", "tile")
MAX_RING = 8


def passed_along(shard, by):
    peers = lax.axis_size(DUCT)
    pairs = [(i, i + by) for i in range(peers) if 0 <= i + by < peers]
    return lax.ppermute(shard, DUCT, pairs)


def own_coarse_rows(coarse_inverse):
    rows = lax.all_to_all(coarse_inverse, "sub", split_axis=0, concat_axis=3, tiled=True)
    rows = lax.all_gather(rows, "rep", axis=2, tiled=True)
    return rows.reshape(rows.shape[2], rows.shape[3] * rows.shape[4])


def gathered(projected, up_trace, low_trace):
    peers = lax.axis_size(DUCT)
    rows = projected.shape[0]
    if peers > MAX_RING:
        vector = lax.all_gather(projected, DUCT, axis=0, tiled=True)
        if up_trace is None:
            return (vector, None, None)
        return (vector, passed_along(up_trace, 1), passed_along(low_trace, -1))
    parts = [projected]
    extras = {}
    if up_trace is not None:
        extras.setdefault(1, []).append(up_trace)
        extras.setdefault(peers - 1, []).append(low_trace)
    came = {}
    for k in range(1, peers):
        piece = jnp.concatenate([projected] + extras.get(k, []), axis=0)
        got = lax.ppermute(piece, DUCT, [(i, (i + k) % peers) for i in range(peers)])
        parts.append(got[:rows])
        came[k] = got[rows:]
    vector = jnp.concatenate(parts, axis=0)
    if up_trace is None:
        return (vector, None, None)
    from_lower = came[1][: up_trace.shape[0]]
    from_upper = came[peers - 1][came[peers - 1].shape[0] - low_trace.shape[0] :]
    return (vector, from_lower, from_upper)


def block_order(matrix):
    peers = lax.axis_size(DUCT)
    if peers > MAX_RING:
        return matrix
    came_from = (lax.axis_index(DUCT) - jnp.arange(peers)) % peers
    blocks = matrix.reshape(matrix.shape[0], peers, -1)
    return jnp.take(blocks, came_from, axis=1).reshape(matrix.shape)


def local(
    right_side,
    interface_inverse,
    coupling,
    trace_rows,
    deflation_basis,
    deflation_counts,
    coarse_inverse,
):
    source = right_side[0]
    inverse = interface_inverse[0]
    iface_rows = inverse.shape[0]
    face_rows = coupling.shape[2]
    slot_count = deflation_basis.shape[2]
    peers = lax.axis_size(DUCT)
    position = lax.axis_index(DUCT)
    slot_ids = jnp.arange(slot_count, dtype=jnp.int32)
    masked_basis = jnp.where(
        slot_ids[None, :] < deflation_counts[0],
        deflation_basis[0],
        jnp.zeros((), deflation_basis.dtype),
    )
    lower_rows_at = trace_rows[0, 0]
    upper_rows_at = trace_rows[0, 1]
    coarse_rows = own_coarse_rows(coarse_inverse)
    width = coarse_rows.shape[1]
    below = passed_along(jnp.concatenate([coarse_rows, masked_basis[upper_rows_at]], axis=1), 1)
    above = passed_along(jnp.concatenate([coarse_rows, masked_basis[lower_rows_at]], axis=1), -1)
    coarse_all = block_order(
        jnp.concatenate([coarse_rows, below[:, :width], above[:, :width]], axis=0)
    )
    below_basis = below[:, width:]
    above_basis = above[:, width:]
    has_lower = position > 0
    has_upper = position < peers - 1
    lower_gain = coupling[0, 0][:, None]
    upper_gain = coupling[0, 1][:, None]
    block = coarse_rows.shape[0]
    iterate = None
    boundary = source
    for cycle_index in range(ROUNDS):
        local_solve = jnp.dot(inverse, boundary, preferred_element_type=jnp.float32)
        if iterate is None:
            defect = local_solve.astype(jnp.bfloat16)
        else:
            defect = (local_solve - iterate).astype(jnp.bfloat16)
        projected = lax.dot_general(
            masked_basis, defect, (((0,), (0,)), ((), ())), preferred_element_type=jnp.float32
        ).astype(jnp.bfloat16)
        last = cycle_index == ROUNDS - 1
        if last:
            vector = gathered(projected, None, None)[0]
            coarse = jnp.dot(coarse_all[:block], vector, preferred_element_type=jnp.float32)
            coarse = coarse.astype(jnp.bfloat16)
            iterate = local_solve + jnp.dot(
                masked_basis, coarse, preferred_element_type=jnp.float32
            )
            break
        vector, solve_lower, solve_upper = gathered(
            projected,
            local_solve[upper_rows_at].astype(jnp.bfloat16),
            local_solve[lower_rows_at].astype(jnp.bfloat16),
        )
        coarse = jnp.dot(coarse_all, vector, preferred_element_type=jnp.float32).astype(
            jnp.bfloat16
        )
        iterate = local_solve + jnp.dot(
            masked_basis, coarse[:block], preferred_element_type=jnp.float32
        )
        from_lower = solve_lower.astype(jnp.float32) + jnp.dot(
            below_basis, coarse[block : 2 * block], preferred_element_type=jnp.float32
        )
        from_upper = solve_upper.astype(jnp.float32) + jnp.dot(
            above_basis, coarse[2 * block :], preferred_element_type=jnp.float32
        )
        from_lower = jnp.where(has_lower, from_lower, 0.0)
        from_upper = jnp.where(has_upper, from_upper, 0.0)
        lower_rows = source[:face_rows].astype(jnp.float32) + lower_gain * from_lower
        upper_rows = source[iface_rows - face_rows :].astype(jnp.float32) + upper_gain * from_upper
        boundary = jnp.concatenate(
            [
                lower_rows.astype(jnp.bfloat16),
                source[face_rows : iface_rows - face_rows],
                upper_rows.astype(jnp.bfloat16),
            ],
            axis=0,
        )
    return iterate.astype(jnp.bfloat16)[None]


def solution(mesh):
    placed = (
        P(("group", "sub", "tile"), None, "rep"),
        P(("group", "sub", "tile"), None, None),
        P(("group", "sub", "tile"), None, None),
        P(("group", "sub", "tile"), None, None),
        P(("group", "sub", "tile"), None, None),
        P(("group", "sub", "tile")),
        P("group", "tile", "rep", "sub", None),
    )
    return jax.shard_map(
        local,
        mesh=mesh,
        in_specs=placed,
        out_specs=P(("group", "sub", "tile"), None, "rep"),
        check_vma=False,
    )
```

profile of v0, /device:TPU:0, one launch (start us, length us, event | category | flops | bytes accessed | tf_op | source)
XLA Modules:
  0.0 113.9 jit_solution(484941452803717135)
XLA Ops:
  1.8 1.8 %fusion.2 = f32[1024,256]{1,0:T(8,128)S(1)} fusion(bf16[1,1024,1024]{2,1,0:T(8,128)(2,1)S(1)} %copy-done, bf16[1,1024,256]{2,1,0:T(8,128)(2,1)} %param.7), kind=kOutput, calls=%fused_computation.7 | convolution fusion | flops 536870912 | bytes 3670016 | tf_op jit(solution)/shard_map/dot_general | solution.py:100
  4.5 3.0 %collective-permute-start.3 = (bf16[128,256]{1,0:T(8,128)(2,1)}, bf16[128,256]{1,0:T(8,128)(2,1)}, u32[]{:S(2)}, u32[]{:S(2)}) collective-permute-start(bf16[128,256]{1,0:T(8,128)(2,1)} %get-tuple-element.14), channel_id=1, source_target_pairs={{0,4},{2,6},{4,8},{6,10},{8,12},{10,14},{12,0},{14,2},{1,5},{3,7},... | collective-permute-start | bytes 196616 | tf_op jit(solution)/shard_map/ppermute | solution.py:39
  7.5 2.5 %collective-permute-start.4 = (bf16[128,256]{1,0:T(8,128)(2,1)}, bf16[128,256]{1,0:T(8,128)(2,1)}, u32[]{:S(2)}, u32[]{:S(2)}) collective-permute-start(bf16[128,256]{1,0:T(8,128)(2,1)} %get-tuple-element.14), channel_id=1, source_target_pairs={{0,6},{2,8},{4,10},{6,12},{8,14},{10,0},{12,2},{14,4},{1,7},{3,9},... | collective-permute-start | bytes 196616 | tf_op jit(solution)/shard_map/ppermute | solution.py:39
  11.3 2.7 %collective-permute-start.6 = (bf16[128,256]{1,0:T(8,128)(2,1)}, bf16[128,256]{1,0:T(8,128)(2,1)}, u32[]{:S(2)}, u32[]{:S(2)}) collective-permute-start(bf16[128,256]{1,0:T(8,128)(2,1)} %get-tuple-element.14), channel_id=1, source_target_pairs={{0,10},{2,12},{4,14},{6,0},{8,2},{10,4},{12,6},{14,8},{1,11},{3,13... | collective-permute-start | bytes 196616 | tf_op jit(solution)/shard_map/ppermute | solution.py:39
  14.0 3.3 %all-to-all-start = ((bf16[4,1,64,1,256]{4,2,3,1,0:T(8,128)(2,1)}), bf16[4,1,64,1,256]{4,2,3,1,0:T(8,128)(2,1)S(1)}, u32[]{:S(2)}, u32[]{:S(2)}) async-start(bf16[4,1,64,1,256]{4,2,3,1,0:T(8,128)(2,1)} %param.13), calls=%async_computation | async-start | bytes 262144 | tf_op jit(solution)/shard_map/all_to_all | solution.py:18
  20.1 1.6 %pad_maximum_fusion.3 = (bf16[256,256]{1,0:T(8,128)(2,1)}, bf16[256,256]{1,0:T(8,128)(2,1)}) fusion(bf16[128,256]{1,0:T(8,128)(2,1)} %get-tuple-element.14, bf16[128,256]{1,0:T(8,128)(2,1)} %gather_fusion.4, bf16[128,256]{1,0:T(8,128)(2,1)} %gather_fusion), kind=kLoop, calls=%fused_computation.35 | loop fusion | flops 458752 | bytes 458752 | tf_op jit(solution)/shard_map/concatenate | solution.py:38
  23.2 1.8 %slice_bitcast_fusion = bf16[768,256]{1,0:T(8,128)(2,1)} fusion(bf16[1,1024,256]{2,1,0:T(8,128)(2,1)} %param.7), kind=kLoop, calls=%fused_computation.30 | loop fusion | bytes 786432 | tf_op jit(solution)/shard_map/slice | solution.py:141
  31.3 3.8 %collective-permute-start.7 = (bf16[128,256]{1,0:T(8,128)(2,1)}, bf16[128,256]{1,0:T(8,128)(2,1)}, u32[]{:S(2)}, u32[]{:S(2)}) collective-permute-start(bf16[128,256]{1,0:T(8,128)(2,1)} %get-tuple-element.14), channel_id=1, source_target_pairs={{0,12},{2,14},{4,0},{6,2},{8,4},{10,6},{12,8},{14,10},{1,13},{3,15... | collective-permute-start | bytes 196616 | tf_op jit(solution)/shard_map/ppermute | solution.py:39
  44.0 2.1 %all-gather = bf16[1,1,128,4,1,256]{5,3,4,1,0,2:T(4,128)(2,1)} all-gather(bf16[1,1,64,4,1,256]{5,3,4,1,0,2:T(4,128)(2,1)S(1)} %copy.23), channel_id=2, replica_groups=mesh['group'=2,'sub'=4,'tile'=2,'rep'=2] {'rep'}, dimensions={2}, use_global_device_ids=true | all-gather | bytes 393216 | tf_op jit(solution)/shard_map/all_gather | solution.py:19
  46.2 1.8 %copy.24 = bf16[1,1,128,4,1,256]{2,5,3,4,1,0:T(8,128)(2,1)} copy(bf16[1,1,128,4,1,256]{5,3,4,1,0,2:T(4,128)(2,1)} %all-gather) | data formatting | bytes 524288 | tf_op jit(solution)/shard_map/all_gather | solution.py:19
  48.0 1.9 %pad_maximum_fusion.1 = (bf16[128,1152]{0,1:T(8,128)(2,1)}, bf16[128,1152]{0,1:T(8,128)(2,1)}) fusion(bf16[128,128]{0,1:T(8,128)(2,1)} %copy.25, bf16[128,1024]{0,1:T(8,128)(2,1)} %bitcast.63, bf16[128,128]{0,1:T(8,128)(2,1)} %copy.27), kind=kLoop, calls=%fused_computation.31 | loop fusion | flops 1032192 | bytes 917504 | tf_op jit(solution)/shard_map/concatenate | solution.py:85
  51.1 5.3 %collective-permute-start.1 = (bf16[128,1152]{0,1:T(8,128)(2,1)}, bf16[128,1152]{0,1:T(8,128)(2,1)}, u32[]{:S(2)}, u32[]{:S(2)}) collective-permute-start(bf16[128,1152]{0,1:T(8,128)(2,1)} %get-tuple-element.5), channel_id=1, source_target_pairs={{0,2},{2,4},{4,6},{6,8},{8,10},{10,12},{12,14},{1,3},{3,5},{5,7},{... | collective-permute-start | bytes 884744 | tf_op jit(solution)/shard_map/ppermute | solution.py:14
  59.4 1.8 %copy.28 = bf16[128,8,128]{2,0,1:T(8,128)(2,1)} copy(bf16[128,8,128]{0,2,1:T(8,128)(2,1)} %bitcast.64) | data formatting | bytes 524288 | tf_op jit(solution)/shard_map/concatenate | solution.py:88
  61.2 1.7 %slice.99 = bf16[128,1024]{0,1:T(8,128)(2,1)} slice(bf16[128,1152]{0,1:T(8,128)(2,1)} %collective-permute-done.2), slice={[0:128], [0:1024]} | slice | bytes 524288 | tf_op jit(solution)/shard_map/slice | solution.py:88
  62.8 1.8 %copy.30 = bf16[128,8,128]{2,0,1:T(8,128)(2,1)} copy(bf16[128,8,128]{0,2,1:T(8,128)(2,1)} %bitcast.66) | data formatting | bytes 524288 | tf_op jit(solution)/shard_map/concatenate | solution.py:88
  64.6 1.8 %collective-permute-done.1 = bf16[128,1152]{0,1:T(8,128)(2,1)} collective-permute-done((bf16[128,1152]{0,1:T(8,128)(2,1)}, bf16[128,1152]{0,1:T(8,128)(2,1)}, u32[]{:S(2)}, u32[]{:S(2)}) %collective-permute-start.1) | collective-permute-done | bytes 294944 | tf_op jit(solution)/shard_map/ppermute | solution.py:14
  66.4 1.7 %slice.98 = bf16[128,1024]{0,1:T(8,128)(2,1)} slice(bf16[128,1152]{0,1:T(8,128)(2,1)} %collective-permute-done.1), slice={[0:128], [0:1024]} | slice | bytes 524288 | tf_op jit(solution)/shard_map/slice | solution.py:88
  68.1 1.8 %copy.29 = bf16[128,8,128]{2,0,1:T(8,128)(2,1)} copy(bf16[128,8,128]{0,2,1:T(8,128)(2,1)} %bitcast.67) | data formatting | bytes 524288 | tf_op jit(solution)/shard_map/concatenate | solution.py:88
  69.9 2.1 %pad_maximum_fusion = bf16[384,8,128]{2,0,1:T(8,128)(2,1)} fusion(bf16[128,8,128]{2,0,1:T(8,128)(2,1)} %copy.30, bf16[128,8,128]{2,0,1:T(8,128)(2,1)} %copy.29, bf16[128,8,128]{2,0,1:T(8,128)(2,1)} %copy.28), kind=kLoop, calls=%fused_computation.21 | loop fusion | flops 2359296 | bytes 1572864 | tf_op jit(solution)/shard_map/concatenate | solution.py:88
  71.9 2.7 %gather_fusion.3 = bf16[8,384,128]{2,1,0:T(8,128)(2,1)} fusion(bf16[384,8,128]{2,0,1:T(8,128)(2,1)} %pad_maximum_fusion, s32[1024]{0:T(1024)S(1)} %pad_clamp_fusion), kind=kCustom, calls=%fused_computation.3 | custom fusion | bytes 1572896 | tf_op jit(solution)/shard_map/jit(_take)/gather | solution.py:56
  74.6 2.3 %copy.31 = bf16[384,8,128]{0,2,1:T(8,128)(2,1)} copy(bf16[384,8,128]{2,0,1:T(8,128)(2,1)} %bitcast.61) | data formatting | bytes 1572864 | tf_op jit(solution)/shard_map/jit(_take)/gather | solution.py:56
  82.1 1.7 %fusion.4 = f32[1024,256]{1,0:T(8,128)} fusion(bf16[1,1024,1024]{2,1,0:T(8,128)(2,1)S(1)} %copy-done, bf16[128,256]{1,0:T(8,128)(2,1)S(1)} %fusion.20, bf16[768,256]{1,0:T(8,128)(2,1)S(1)} %copy-done.2, bf16[128,256]{1,0:T(8,128)(2,1)S(1)} %fusion.21), kind=kOutput, calls=%fused_computation.9 | convolution fusion | flops 538443776 | bytes 3670016 | tf_op jit(solution)/shard_map/dot_general | solution.py:100
  83.8 2.4 %constant_dynamic-update-slice_fusion.13 = (bf16[1024,256]{1,0:T(8,128)(2,1)}, bf16[128,256]{1,0:T(8,128)(2,1)S(1)}) fusion(bf16[1024,128]{1,0:T(8,128)(2,1)S(1)} %bitcast_select_fusion.1, f32[1024,256]{1,0:T(8,128)} %fusion.4, f32[1024,256]{1,0:T(8,128)S(1)} %fusion.2, bf16[384,256]{1,0:T(8,128)(2,1)} %copy-done.3), kind=kOutput, calls=%fused_computation.63 | convolution fusion | flops 135036928 | bytes 2818048 | tf_op jit(solution)/shard_map/dot_general | solution.py:105
  86.2 2.5 %collective-permute-start.9 = (bf16[128,256]{1,0:T(8,128)(2,1)S(1)}, bf16[128,256]{1,0:T(8,128)(2,1)}, u32[]{:S(2)}, u32[]{:S(2)}) collective-permute-start(bf16[128,256]{1,0:T(8,128)(2,1)S(1)} %get-tuple-element.16), channel_id=1, source_target_pairs={{0,2},{2,4},{4,6},{6,8},{8,10},{10,12},{12,14},{14,0},{1,3},{3,5},... | collective-permute-start | bytes 196616 | tf_op jit(solution)/shard_map/ppermute | solution.py:39
  88.7 1.7 %slice_select_fusion = bf16[128,8,128]{2,0,1:T(8,128)(2,1)} fusion(bf16[384,8,128]{2,0,1:T(8,128)(2,1)} %bitcast.62, pred[8]{0:T(512)(128)(4,1)S(1)} %copy-done.7), kind=kLoop, calls=%fused_computation.33 | loop fusion | flops 131072 | bytes 524296 | tf_op jit(solution)/shard_map/jit(_take)/select_n | solution.py:56
  90.5 2.1 %collective-permute-start.10 = (bf16[128,256]{1,0:T(8,128)(2,1)S(1)}, bf16[128,256]{1,0:T(8,128)(2,1)}, u32[]{:S(2)}, u32[]{:S(2)}) collective-permute-start(bf16[128,256]{1,0:T(8,128)(2,1)S(1)} %get-tuple-element.16), channel_id=1, source_target_pairs={{0,4},{2,6},{4,8},{6,10},{8,12},{10,14},{12,0},{14,2},{1,5},{3,7},... | collective-permute-start | bytes 196616 | tf_op jit(solution)/shard_map/ppermute | solution.py:39
  92.6 2.5 %collective-permute-start.11 = (bf16[128,256]{1,0:T(8,128)(2,1)S(1)}, bf16[128,256]{1,0:T(8,128)(2,1)}, u32[]{:S(2)}, u32[]{:S(2)}) collective-permute-start(bf16[128,256]{1,0:T(8,128)(2,1)S(1)} %get-tuple-element.16), channel_id=1, source_target_pairs={{0,6},{2,8},{4,10},{6,12},{8,14},{10,0},{12,2},{14,4},{1,7},{3,9},... | collective-permute-start | bytes 196616 | tf_op jit(solution)/shard_map/ppermute | solution.py:39
  95.1 2.7 %collective-permute-start.12 = (bf16[128,256]{1,0:T(8,128)(2,1)S(1)}, bf16[128,256]{1,0:T(8,128)(2,1)}, u32[]{:S(2)}, u32[]{:S(2)}) collective-permute-start(bf16[128,256]{1,0:T(8,128)(2,1)S(1)} %get-tuple-element.16), channel_id=1, source_target_pairs={{0,8},{2,10},{4,12},{6,14},{8,0},{10,2},{12,4},{14,6},{1,9},{3,11}... | collective-permute-start | bytes 196616 | tf_op jit(solution)/shard_map/ppermute | solution.py:39
  97.8 1.8 %copy.33 = bf16[128,8,128]{0,2,1:T(8,128)(2,1)} copy(bf16[128,8,128]{2,0,1:T(8,128)(2,1)} %slice_select_fusion) | data formatting | bytes 524288 | tf_op jit(solution)/shard_map/slice | solution.py:111
  99.6 2.4 %collective-permute-start.14 = (bf16[128,256]{1,0:T(8,128)(2,1)S(1)}, bf16[128,256]{1,0:T(8,128)(2,1)S(1)}, u32[]{:S(2)}, u32[]{:S(2)}) collective-permute-start(bf16[128,256]{1,0:T(8,128)(2,1)S(1)} %get-tuple-element.16), channel_id=1, source_target_pairs={{0,12},{2,14},{4,0},{6,2},{8,4},{10,6},{12,8},{14,10},{1,13},{3,15... | collective-permute-start | bytes 196616 | tf_op jit(solution)/shard_map/ppermute | solution.py:39
  103.4 1.6 %collective-permute-start.15 = (bf16[128,256]{1,0:T(8,128)(2,1)S(1)}, bf16[128,256]{1,0:T(8,128)(2,1)S(1)}, u32[]{:S(2)}, u32[]{:S(2)}) collective-permute-start(bf16[128,256]{1,0:T(8,128)(2,1)S(1)} %get-tuple-element.16), channel_id=1, source_target_pairs={{0,14},{2,0},{4,2},{6,4},{8,6},{10,8},{12,10},{14,12},{1,15},{3,1}... | collective-permute-start | bytes 196616 | tf_op jit(solution)/shard_map/ppermute | solution.py:39
  111.4 2.6 %fusion.10 = bf16[1,1024,256]{2,1,0:T(8,128)(2,1)} fusion(f32[1024,256]{1,0:T(8,128)S(1)} %copy-done.1, bf16[1024,128]{1,0:T(8,128)(2,1)S(1)} %bitcast_select_fusion.1, bf16[128,1024]{0,1:T(8,128)(2,1)} %bitcast.65, bf16[1024,256]{1,0:T(8,128)(2,1)} %constant_dynamic-update-slice_fusion.6), kind=kOutput, calls=%fused_computation.15 | convolution fusion | flops 134774784 | bytes 2621440 | tf_op jit(solution)/shard_map/dot_general | solution.py:113
  (76 shorter events, 39.7 us)
Async XLA Ops:
  0.0 1.8 %copy-start = (bf16[1,1024,1024]{2,1,0:T(8,128)(2,1)S(1)}, bf16[1,1024,1024]{2,1,0:T(8,128)(2,1)}, u32[]{:S(2)}) copy-start(bf16[1,1024,1024]{2,1,0:T(8,128)(2,1)} %param.8) | copy-start | bytes 6291460
  1.8 15.5 %copy-start.4 = (s32[1,2,128]{2,1,0:T(2,128)S(1)}, s32[1,2,128]{2,1,0:T(2,128)}, u32[]{:S(2)}) copy-start(s32[1,2,128]{2,1,0:T(2,128)} %param.10) | copy-start | bytes 3076
  3.6 21.5 %copy-start.5 = (f32[1,2,128]{2,1,0:T(2,128)S(1)}, f32[1,2,128]{2,1,0:T(2,128)}, u32[]{:S(2)}) copy-start(f32[1,2,128]{2,1,0:T(2,128)} %param.9) | copy-start | bytes 3076
  4.5 32.0 %collective-permute-start.3 = (bf16[128,256]{1,0:T(8,128)(2,1)}, bf16[128,256]{1,0:T(8,128)(2,1)}, u32[]{:S(2)}, u32[]{:S(2)}) collective-permute-start(bf16[128,256]{1,0:T(8,128)(2,1)} %get-tuple-element.14), channel_id=1, source_target_pairs={{0,4},{2,6},{4,8},{6,10},{8,12},{10,14},{12,0},{14,2},{1,5},{3,7},... | collective-permute-start | bytes 196616 | tf_op jit(solution)/shard_map/ppermute | solution.py:39
  7.5 31.9 %collective-permute-start.4 = (bf16[128,256]{1,0:T(8,128)(2,1)}, bf16[128,256]{1,0:T(8,128)(2,1)}, u32[]{:S(2)}, u32[]{:S(2)}) collective-permute-start(bf16[128,256]{1,0:T(8,128)(2,1)} %get-tuple-element.14), channel_id=1, source_target_pairs={{0,6},{2,8},{4,10},{6,12},{8,14},{10,0},{12,2},{14,4},{1,7},{3,9},... | collective-permute-start | bytes 196616 | tf_op jit(solution)/shard_map/ppermute | solution.py:39
  10.1 30.9 %collective-permute-start.5 = (bf16[128,256]{1,0:T(8,128)(2,1)}, bf16[128,256]{1,0:T(8,128)(2,1)}, u32[]{:S(2)}, u32[]{:S(2)}) collective-permute-start(bf16[128,256]{1,0:T(8,128)(2,1)} %get-tuple-element.14), channel_id=1, source_target_pairs={{0,8},{2,10},{4,12},{6,14},{8,0},{10,2},{12,4},{14,6},{1,9},{3,11}... | collective-permute-start | bytes 196616 | tf_op jit(solution)/shard_map/ppermute | solution.py:39
  11.3 31.2 %collective-permute-start.6 = (bf16[128,256]{1,0:T(8,128)(2,1)}, bf16[128,256]{1,0:T(8,128)(2,1)}, u32[]{:S(2)}, u32[]{:S(2)}) collective-permute-start(bf16[128,256]{1,0:T(8,128)(2,1)} %get-tuple-element.14), channel_id=1, source_target_pairs={{0,10},{2,12},{4,14},{6,0},{8,2},{10,4},{12,6},{14,8},{1,11},{3,13... | collective-permute-start | bytes 196616 | tf_op jit(solution)/shard_map/ppermute | solution.py:39
  14.0 30.0 %all-to-all-start = ((bf16[4,1,64,1,256]{4,2,3,1,0:T(8,128)(2,1)}), bf16[4,1,64,1,256]{4,2,3,1,0:T(8,128)(2,1)S(1)}, u32[]{:S(2)}, u32[]{:S(2)}) async-start(bf16[4,1,64,1,256]{4,2,3,1,0:T(8,128)(2,1)} %param.13), calls=%async_computation | async-start | bytes 262144 | tf_op jit(solution)/shard_map/all_to_all | solution.py:18
  21.7 9.5 %collective-permute-start = (bf16[256,256]{1,0:T(8,128)(2,1)}, bf16[256,256]{1,0:T(8,128)(2,1)}, u32[]{:S(2)}, u32[]{:S(2)}) collective-permute-start(bf16[256,256]{1,0:T(8,128)(2,1)} %get-tuple-element.8), channel_id=1, source_target_pairs={{0,2},{2,4},{4,6},{6,8},{8,10},{10,12},{12,14},{14,0},{1,3},{3,5},... | collective-permute-start | bytes 393224 | tf_op jit(solution)/shard_map/ppermute | solution.py:39
  25.0 0.7 copy-start.6
  31.3 25.2 %collective-permute-start.7 = (bf16[128,256]{1,0:T(8,128)(2,1)}, bf16[128,256]{1,0:T(8,128)(2,1)}, u32[]{:S(2)}, u32[]{:S(2)}) collective-permute-start(bf16[128,256]{1,0:T(8,128)(2,1)} %get-tuple-element.14), channel_id=1, source_target_pairs={{0,12},{2,14},{4,0},{6,2},{8,4},{10,6},{12,8},{14,10},{1,13},{3,15... | collective-permute-start | bytes 196616 | tf_op jit(solution)/shard_map/ppermute | solution.py:39
  36.6 21.3 %collective-permute-start.8 = (bf16[256,256]{1,0:T(8,128)(2,1)}, bf16[256,256]{1,0:T(8,128)(2,1)}, u32[]{:S(2)}, u32[]{:S(2)}) collective-permute-start(bf16[256,256]{1,0:T(8,128)(2,1)} %get-tuple-element.7), channel_id=1, source_target_pairs={{0,14},{2,0},{4,2},{6,4},{8,6},{10,8},{12,10},{14,12},{1,15},{3,1}... | collective-permute-start | bytes 393224 | tf_op jit(solution)/shard_map/ppermute | solution.py:39
  49.8 11.3 %collective-permute-start.2 = (bf16[128,1152]{0,1:T(8,128)(2,1)}, bf16[128,1152]{0,1:T(8,128)(2,1)}, u32[]{:S(2)}, u32[]{:S(2)}) collective-permute-start(bf16[128,1152]{0,1:T(8,128)(2,1)} %get-tuple-element.6), channel_id=1, source_target_pairs={{2,0},{4,2},{6,4},{8,6},{10,8},{12,10},{14,12},{3,1},{5,3},{7,5},{... | collective-permute-start | bytes 884744 | tf_op jit(solution)/shard_map/ppermute | solution.py:14
  51.1 15.3 %collective-permute-start.1 = (bf16[128,1152]{0,1:T(8,128)(2,1)}, bf16[128,1152]{0,1:T(8,128)(2,1)}, u32[]{:S(2)}, u32[]{:S(2)}) collective-permute-start(bf16[128,1152]{0,1:T(8,128)(2,1)} %get-tuple-element.5), channel_id=1, source_target_pairs={{0,2},{2,4},{4,6},{6,8},{8,10},{10,12},{12,14},{1,3},{3,5},{5,7},{... | collective-permute-start | bytes 884744 | tf_op jit(solution)/shard_map/ppermute | solution.py:14
  76.9 2.9 %copy-start.9 = (f32[128]{0:T(128)S(1)}, f32[128]{0:T(128)}, u32[]{:S(2)}) copy-start(f32[128]{0:T(128)} %get-tuple-element.10) | copy-start | bytes 1540
  76.9 4.1 %copy-start.8 = (f32[128]{0:T(128)S(1)}, f32[128]{0:T(128)}, u32[]{:S(2)}) copy-start(f32[128]{0:T(128)} %get-tuple-element.9) | copy-start | bytes 1540
  76.9 5.2 %copy-start.2 = (bf16[768,256]{1,0:T(8,128)(2,1)S(1)}, bf16[768,256]{1,0:T(8,128)(2,1)}, u32[]{:S(2)}) copy-start(bf16[768,256]{1,0:T(8,128)(2,1)} %slice_bitcast_fusion) | copy-start | bytes 1179652
  79.8 1.2 %copy-start.3 = (bf16[384,256]{1,0:T(8,128)(2,1)}, bf16[384,256]{1,0:T(8,128)(2,1)S(1)}, u32[]{:S(2)}) copy-start(bf16[384,256]{1,0:T(8,128)(2,1)S(1)} %convolution_convert_fusion) | copy-start | bytes 589828
  83.8 4.9 %copy-start.7 = (pred[8]{0:T(512)(128)(4,1)S(1)}, pred[8]{0:T(512)(128)(4,1)}, u32[]{:S(2)}) copy-start(pred[8]{0:T(512)(128)(4,1)} %copy-done.6) | copy-start | bytes 28
  86.2 25.1 %copy-start.1 = (f32[1024,256]{1,0:T(8,128)S(1)}, f32[1024,256]{1,0:T(8,128)}, u32[]{:S(2)}) copy-start(f32[1024,256]{1,0:T(8,128)} %fusion.4) | copy-start | bytes 3145732
  86.2 13.3 %collective-permute-start.9 = (bf16[128,256]{1,0:T(8,128)(2,1)S(1)}, bf16[128,256]{1,0:T(8,128)(2,1)}, u32[]{:S(2)}, u32[]{:S(2)}) collective-permute-start(bf16[128,256]{1,0:T(8,128)(2,1)S(1)} %get-tuple-element.16), channel_id=1, source_target_pairs={{0,2},{2,4},{4,6},{6,8},{8,10},{10,12},{12,14},{14,0},{1,3},{3,5},... | collective-permute-start | bytes 196616 | tf_op jit(solution)/shard_map/ppermute | solution.py:39
  90.5 12.9 %collective-permute-start.10 = (bf16[128,256]{1,0:T(8,128)(2,1)S(1)}, bf16[128,256]{1,0:T(8,128)(2,1)}, u32[]{:S(2)}, u32[]{:S(2)}) collective-permute-start(bf16[128,256]{1,0:T(8,128)(2,1)S(1)} %get-tuple-element.16), channel_id=1, source_target_pairs={{0,4},{2,6},{4,8},{6,10},{8,12},{10,14},{12,0},{14,2},{1,5},{3,7},... | collective-permute-start | bytes 196616 | tf_op jit(solution)/shard_map/ppermute | solution.py:39
  92.6 13.9 %collective-permute-start.11 = (bf16[128,256]{1,0:T(8,128)(2,1)S(1)}, bf16[128,256]{1,0:T(8,128)(2,1)}, u32[]{:S(2)}, u32[]{:S(2)}) collective-permute-start(bf16[128,256]{1,0:T(8,128)(2,1)S(1)} %get-tuple-element.16), channel_id=1, source_target_pairs={{0,6},{2,8},{4,10},{6,12},{8,14},{10,0},{12,2},{14,4},{1,7},{3,9},... | collective-permute-start | bytes 196616 | tf_op jit(solution)/shard_map/ppermute | solution.py:39
  95.1 12.9 %collective-permute-start.12 = (bf16[128,256]{1,0:T(8,128)(2,1)S(1)}, bf16[128,256]{1,0:T(8,128)(2,1)}, u32[]{:S(2)}, u32[]{:S(2)}) collective-permute-start(bf16[128,256]{1,0:T(8,128)(2,1)S(1)} %get-tuple-element.16), channel_id=1, source_target_pairs={{0,8},{2,10},{4,12},{6,14},{8,0},{10,2},{12,4},{14,6},{1,9},{3,11}... | collective-permute-start | bytes 196616 | tf_op jit(solution)/shard_map/ppermute | solution.py:39
  97.8 11.7 %collective-permute-start.13 = (bf16[128,256]{1,0:T(8,128)(2,1)S(1)}, bf16[128,256]{1,0:T(8,128)(2,1)S(1)}, u32[]{:S(2)}, u32[]{:S(2)}) collective-permute-start(bf16[128,256]{1,0:T(8,128)(2,1)S(1)} %get-tuple-element.16), channel_id=1, source_target_pairs={{0,10},{2,12},{4,14},{6,0},{8,2},{10,4},{12,6},{14,8},{1,11},{3,13... | collective-permute-start | bytes 196616 | tf_op jit(solution)/shard_map/ppermute | solution.py:39
  99.6 10.5 %collective-permute-start.14 = (bf16[128,256]{1,0:T(8,128)(2,1)S(1)}, bf16[128,256]{1,0:T(8,128)(2,1)S(1)}, u32[]{:S(2)}, u32[]{:S(2)}) collective-permute-start(bf16[128,256]{1,0:T(8,128)(2,1)S(1)} %get-tuple-element.16), channel_id=1, source_target_pairs={{0,12},{2,14},{4,0},{6,2},{8,4},{10,6},{12,8},{14,10},{1,13},{3,15... | collective-permute-start | bytes 196616 | tf_op jit(solution)/shard_map/ppermute | solution.py:39
  103.4 7.3 %collective-permute-start.15 = (bf16[128,256]{1,0:T(8,128)(2,1)S(1)}, bf16[128,256]{1,0:T(8,128)(2,1)S(1)}, u32[]{:S(2)}, u32[]{:S(2)}) collective-permute-start(bf16[128,256]{1,0:T(8,128)(2,1)S(1)} %get-tuple-element.16), channel_id=1, source_target_pairs={{0,14},{2,0},{4,2},{6,4},{8,6},{10,8},{12,10},{14,12},{1,15},{3,1}... | collective-permute-start | bytes 196616 | tf_op jit(solution)/shard_map/ppermute | solution.py:39
where the time goes:
time: 116 us; the launch traced here: 114 us
  local copies, waits for them, and re-layouts  46.3 us (40%)
  starting transfers between devices  39.9 us (34%)
  matrix products  13.1 us (11%)
  other arithmetic  9.73 us (8%)
  blocking collectives  2.13 us (2%)
  waiting for transfers between devices  1.86 us (2%)
    ppermute x14, starting transfers between devices, gathered(): lax.ppermute(piece, DUCT, [(i, (i + k) % peers) for i in range(peers)])  30 us
    unnamed x32, local copies, waits for them, and re-layouts  16 us
    ppermute x2, starting transfers between devices, passed_along(): return lax.ppermute(shard, DUCT, pairs)  6.56 us
    concatenate x3, local copies, waits for them, and re-layouts, local(): jnp.concatenate([coarse_rows, below[:, :width], above[:, :width]], axis=0)  5.36 us
    gather x2, local copies, waits for them, and re-layouts, block_order(): return jnp.take(blocks, came_from, axis=1).reshape(matrix.shape)  4.98 us
    dot_general x2, matrix products, local(): local_solve = jnp.dot(inverse, boundary, preferred_element_type=jnp.float32)  3.46 us
    dot_general x2, matrix products, local(): lax.dot_general(masked_basis, defect, (((0,), (0,)), ((), ())), preferred...  3.35 us
    all_to_all x1, starting transfers between devices, own_coarse_rows(): lax.all_to_all(coarse_inverse, 'sub', split_axis=0, concat_axis=3, tiled=...  3.33 us
  transfers between devices with their start and end apart: 17, of which 1 were waited for; matrix products, arithmetic and copies ran while one was open for 37% of the time, Pallas kernels for 0%

commit v1 on v0

--- a/solution.py
+++ b/solution.py
@@ -8,6 +8,17 @@
 MAX_RING = 8
 
 
+def cut_along(x, dim, size):
+    before, after = (x.shape[:dim], x.shape[dim + 1 :])
+    return jnp.moveaxis(x.reshape(*before, size, -1, *after), dim, 0)
+
+
+def laid_out(parts, dim):
+    parts = jnp.moveaxis(parts, 0, dim)
+    dims = parts.shape
+    return parts.reshape(*dims[:dim], dims[dim] * dims[dim + 1], *dims[dim + 2 :])
+
+
 def passed_along(shard, by):
     peers = lax.axis_size(DUCT)
     pairs = [(i, i + by) for i in range(peers) if 0 <= i + by < peers]
@@ -15,7 +26,16 @@
 
 
 def own_coarse_rows(coarse_inverse):
-    rows = lax.all_to_all(coarse_inverse, "sub", split_axis=0, concat_axis=3, tiled=True)
+    peers_2, index = (lax.axis_size("sub"), lax.axis_index("sub"))
+    tiles = cut_along(coarse_inverse, 0, peers_2)
+    outs = [tiles[index]]
+    for lap in range(1, peers_2):
+        sent = tiles[(index + lap) % peers_2]
+        outs.append(
+            lax.ppermute(sent, "sub", [(i_2, (i_2 + lap) % peers_2) for i_2 in range(peers_2)])
+        )
+    tiles = jnp.stack(outs)[(index - jnp.arange(peers_2)) % peers_2]
+    rows = laid_out(tiles, 3)
     rows = lax.all_gather(rows, "rep", axis=2, tiled=True)
     return rows.reshape(rows.shape[2], rows.shape[3] * rows.shape[4])
 

time: 116 us -> 111 us (0.957)
  starting transfers between devices: 39.9 us -> 31.9 us
  waiting for transfers between devices: 1.86 us -> 5.63 us
  local copies, waits for them, and re-layouts: 46.3 us -> 43.6 us
  other arithmetic: 9.73 us -> 12.2 us
    ppermute x14, starting transfers between devices: 30 us -> 25.4 us  [gathered(): lax.ppermute(piece, DUCT, [(i, (i + k) % peers) for i in range(peers)])]
    ppermute x2, starting transfers between devices: 6.56 us -> 2.58 us  [passed_along(): return lax.ppermute(shard, DUCT, pairs)]
    ppermute x0 -> x3, starting transfers between devices: none -> 3.94 us  [own_coarse_rows(): lax.ppermute(sent, 'sub', [(i_2, (i_2 + lap) % peers_2) for i_2 in range(...]
    ppermute x2, waiting for transfers between devices: 1.82 us -> 5.58 us  [passed_along(): return lax.ppermute(shard, DUCT, pairs)]
    all_to_all x1 -> x0, starting transfers between devices: 3.33 us -> none  [own_coarse_rows(): lax.all_to_all(coarse_inverse, 'sub', split_axis=0, concat_axis=3, tiled=...]
    another operation x0 -> x1, other arithmetic: none -> 1.47 us  [own_coarse_rows(): tiles = jnp.stack(outs)[(index - jnp.arange(peers_2)) % peers_2]]
    gather x0 -> x1, local copies, waits for them, and re-layouts: none -> 1.46 us  [own_coarse_rows(): tiles = jnp.stack(outs)[(index - jnp.arange(peers_2)) % peers_2]]
    gather x2, local copies, waits for them, and re-layouts: 2.78 us -> 1.42 us  [local(): masked_basis[upper_rows_at]]
  transfers between devices with their start and end apart: 17 -> 19, of which waited for: 1 -> 1; matrix products, arithmetic and copies ran while one was open for 37% -> 38% of each run, Pallas kernels for 0% -> 0%
where the time goes in v1:
time: 111 us; the launch traced here: 110 us
  local copies, waits for them, and re-layouts  43.6 us (39%)
  starting transfers between devices  31.9 us (29%)
  matrix products  13.1 us (12%)
  other arithmetic  12.2 us (11%)
  waiting for transfers between devices  5.63 us (5%)
  blocking collectives  2.13 us (2%)
    ppermute x14, starting transfers between devices, gathered(): lax.ppermute(piece, DUCT, [(i, (i + k) % peers) for i in range(peers)])  25.4 us
    unnamed x42, local copies, waits for them, and re-layouts  15.9 us
    ppermute x2, waiting for transfers between devices, passed_along(): return lax.ppermute(shard, DUCT, pairs)  5.58 us
    concatenate x3, local copies, waits for them, and re-layouts, local(): jnp.concatenate([coarse_rows, below[:, :width], above[:, :width]], axis=0)  5.36 us
    gather x2, local copies, waits for them, and re-layouts, block_order(): return jnp.take(blocks, came_from, axis=1).reshape(matrix.shape)  4.95 us
    ppermute x3, starting transfers between devices, own_coarse_rows(): lax.ppermute(sent, 'sub', [(i_2, (i_2 + lap) % peers_2) for i_2 in range(...  3.94 us
    select_n x3, other arithmetic, block_order(): return jnp.take(blocks, came_from, axis=1).reshape(matrix.shape)  3.72 us
    dot_general x2, matrix products, local(): local_solve = jnp.dot(inverse, boundary, preferred_element_type=jnp.float32)  3.48 us
  transfers between devices with their start and end apart: 19, of which 1 were waited for; matrix products, arithmetic and copies ran while one was open for 38% of the time, Pallas kernels for 0%

profile of v1, /device:TPU:0, one launch (start us, length us, event | category | flops | bytes accessed | tf_op | source)
XLA Modules:
  0.0 109.6 jit_solution(7123039642974546597)
XLA Ops:
  1.8 1.8 %fusion.2 = f32[1024,256]{1,0:T(8,128)S(1)} fusion(bf16[1,1024,1024]{2,1,0:T(8,128)(2,1)S(1)} %copy-done, bf16[1,1024,256]{2,1,0:T(8,128)(2,1)} %param.7), kind=kOutput, calls=%fused_computation.8 | convolution fusion | flops 536870912 | bytes 3670016 | tf_op jit(solution)/shard_map/dot_general | solution.py:120
  4.5 3.0 %collective-permute-start.6 = (bf16[128,256]{1,0:T(8,128)(2,1)}, bf16[128,256]{1,0:T(8,128)(2,1)}, u32[]{:S(2)}, u32[]{:S(2)}) collective-permute-start(bf16[128,256]{1,0:T(8,128)(2,1)} %get-tuple-element.18), channel_id=1, source_target_pairs={{0,4},{2,6},{4,8},{6,10},{8,12},{10,14},{12,0},{14,2},{1,5},{3,7},... | collective-permute-start | bytes 196616 | tf_op jit(solution)/shard_map/ppermute | solution.py:59
  7.6 2.5 %collective-permute-start.7 = (bf16[128,256]{1,0:T(8,128)(2,1)}, bf16[128,256]{1,0:T(8,128)(2,1)}, u32[]{:S(2)}, u32[]{:S(2)}) collective-permute-start(bf16[128,256]{1,0:T(8,128)(2,1)} %get-tuple-element.18), channel_id=1, source_target_pairs={{0,6},{2,8},{4,10},{6,12},{8,14},{10,0},{12,2},{14,4},{1,7},{3,9},... | collective-permute-start | bytes 196616 | tf_op jit(solution)/shard_map/ppermute | solution.py:59
  12.0 2.7 %collective-permute-start.3 = (bf16[1,1,64,1,256]{4,2,3,1,0:T(8,128)(2,1)}, bf16[1,1,64,1,256]{4,2,3,1,0:T(8,128)(2,1)}, u32[]{:S(2)}, u32[]{:S(2)}) collective-permute-start(bf16[1,1,64,1,256]{4,2,3,1,0:T(8,128)(2,1)} %get-tuple-element.9), channel_id=1, source_target_pairs={{0,12},{4,0},{8,4},{12,8},{1,13},{5,1},{9,5},{13,9},{2,14},{6,2},{... | collective-permute-start | bytes 98312 | tf_op jit(solution)/shard_map/ppermute | solution.py:35
  15.3 1.8 %slice_bitcast_fusion = bf16[768,256]{1,0:T(8,128)(2,1)} fusion(bf16[1,1024,256]{2,1,0:T(8,128)(2,1)} %param.7), kind=kLoop, calls=%fused_computation.31 | loop fusion | bytes 786432 | tf_op jit(solution)/shard_map/slice | solution.py:161
  20.5 1.6 %pad_maximum_fusion.3 = (bf16[256,256]{1,0:T(8,128)(2,1)}, bf16[256,256]{1,0:T(8,128)(2,1)}) fusion(bf16[128,256]{1,0:T(8,128)(2,1)} %get-tuple-element.18, bf16[128,256]{1,0:T(8,128)(2,1)S(1)} %gather_fusion.5, bf16[128,256]{1,0:T(8,128)(2,1)S(1)} %gather_fusion), kind=kLoop, calls=%fused_computation.36 | loop fusion | flops 458752 | bytes 458752 | tf_op jit(solution)/shard_map/concatenate | solution.py:58
  27.9 3.0 %collective-permute-start = (bf16[256,256]{1,0:T(8,128)(2,1)}, bf16[256,256]{1,0:T(8,128)(2,1)}, u32[]{:S(2)}, u32[]{:S(2)}) collective-permute-start(bf16[256,256]{1,0:T(8,128)(2,1)} %get-tuple-element.12), channel_id=1, source_target_pairs={{0,2},{2,4},{4,6},{6,8},{8,10},{10,12},{12,14},{14,0},{1,3},{3,5},... | collective-permute-start | bytes 393224 | tf_op jit(solution)/shard_map/ppermute | solution.py:59
  30.9 1.5 %maximum_bitcast_fusion = bf16[4,64,256]{2,1,0:T(8,128)(2,1)} fusion(bf16[1,1,1,64,1,256]{5,3,0,4,2,1:T(8,128)(2,1)} %bitcast.11, bf16[1,1,1,64,1,256]{5,3,0,4,2,1:T(8,128)(2,1)} %bitcast.10, bf16[1,1,1,64,1,256]{5,3,0,4,2,1:T(8,128)(2,1)} %bitcast.9, bf16[1,1,1,64,1,256]{5,3,0,4,2,1:T(8,128)(2,1)} %get-tuple-element.7), kind=kLoop, calls=%fused_computation.38 | loop fusion | flops 196608 | bytes 262144 | tf_op jit(solution)/shard_map/stack | solution.py:37
  33.9 2.1 %all-gather = bf16[1,1,128,4,1,256]{5,2,3,4,1,0:T(8,128)(2,1)} all-gather(bf16[1,1,64,4,1,256]{5,2,3,4,1,0:T(8,128)(2,1)S(1)} %bitcast.77), channel_id=2, replica_groups=mesh['group'=2,'sub'=4,'tile'=2,'rep'=2] {'rep'}, dimensions={2}, use_global_device_ids=true | all-gather | bytes 393216 | tf_op jit(solution)/shard_map/all_gather | solution.py:39
  36.0 1.8 %copy.13 = bf16[1,1,128,4,1,256]{2,5,3,4,1,0:T(8,128)(2,1)} copy(bf16[1,1,128,4,1,256]{5,2,3,4,1,0:T(8,128)(2,1)} %all-gather) | data formatting | bytes 524288 | tf_op jit(solution)/shard_map/all_gather | solution.py:39
  37.8 1.8 %copy.17 = bf16[128,8,128]{2,0,1:T(8,128)(2,1)} copy(bf16[128,8,128]{0,2,1:T(8,128)(2,1)} %bitcast.72) | data formatting | bytes 524288 | tf_op jit(solution)/shard_map/concatenate | solution.py:108
  39.6 1.8 %pad_maximum_fusion.1 = (bf16[128,1152]{0,1:T(8,128)(2,1)S(1)}, bf16[128,1152]{0,1:T(8,128)(2,1)}) fusion(bf16[128,128]{0,1:T(8,128)(2,1)} %copy.14, bf16[128,1024]{0,1:T(8,128)(2,1)} %bitcast.73, bf16[128,128]{0,1:T(8,128)(2,1)} %copy.16), kind=kLoop, calls=%fused_computation.32 | loop fusion | flops 1032192 | bytes 917504 | tf_op jit(solution)/shard_map/concatenate | solution.py:105
  43.7 2.9 %collective-permute-start.11 = (bf16[256,256]{1,0:T(8,128)(2,1)S(1)}, bf16[256,256]{1,0:T(8,128)(2,1)S(1)}, u32[]{:S(2)}, u32[]{:S(2)}) collective-permute-start(bf16[256,256]{1,0:T(8,128)(2,1)S(1)} %copy-done.4), channel_id=1, source_target_pairs={{0,14},{2,0},{4,2},{6,4},{8,6},{10,8},{12,10},{14,12},{1,15},{3,1}... | collective-permute-start | bytes 393224 | tf_op jit(solution)/shard_map/ppermute | solution.py:59
  46.6 1.5 %constant_dynamic-update-slice_fusion.4 = bf16[1024,256]{1,0:T(8,128)(2,1)} fusion(bf16[1024,256]{1,0:T(8,128)(2,1)} %slice_dynamic-update-slice_fusion.1, bf16[128,256]{1,0:T(8,128)(2,1)} %collective-permute-done.6), kind=kLoop, calls=%fused_computation.56 | loop fusion | bytes 131072
  49.4 1.5 %constant_dynamic-update-slice_fusion.3 = bf16[1024,256]{1,0:T(8,128)(2,1)} fusion(bf16[1024,256]{1,0:T(8,128)(2,1)} %constant_dynamic-update-slice_fusion.4, bf16[128,256]{1,0:T(8,128)(2,1)} %collective-permute-done.7), kind=kLoop, calls=%fused_computation.55 | loop fusion | bytes 131072
  52.1 1.5 %constant_dynamic-update-slice_fusion.2 = bf16[1024,256]{1,0:T(8,128)(2,1)} fusion(bf16[1024,256]{1,0:T(8,128)(2,1)} %constant_dynamic-update-slice_fusion.3, bf16[128,256]{1,0:T(8,128)(2,1)} %collective-permute-done.8), kind=kLoop, calls=%fused_computation.54 | loop fusion | bytes 131072
  53.6 1.5 %constant_dynamic-update-slice_fusion.1 = bf16[1024,256]{1,0:T(8,128)(2,1)} fusion(bf16[1024,256]{1,0:T(8,128)(2,1)} %constant_dynamic-update-slice_fusion.2, bf16[128,256]{1,0:T(8,128)(2,1)} %collective-permute-done.9), kind=kLoop, calls=%fused_computation.53 | loop fusion | bytes 131072
  56.4 5.6 %collective-permute-done.4 = bf16[128,1152]{0,1:T(8,128)(2,1)S(1)} collective-permute-done((bf16[128,1152]{0,1:T(8,128)(2,1)S(1)}, bf16[128,1152]{0,1:T(8,128)(2,1)S(1)}, u32[]{:S(2)}, u32[]{:S(2)}) %collective-permute-start.4) | collective-permute-done | bytes 294944 | tf_op jit(solution)/shard_map/ppermute | solution.py:25
  63.4 1.8 %copy.18 = bf16[128,8,128]{2,0,1:T(8,128)(2,1)} copy(bf16[128,8,128]{0,2,1:T(8,128)(2,1)} %bitcast.75) | data formatting | bytes 524288 | tf_op jit(solution)/shard_map/concatenate | solution.py:108
  65.2 1.7 %slice.101 = bf16[128,1024]{0,1:T(8,128)(2,1)} slice(bf16[128,1152]{0,1:T(8,128)(2,1)} %collective-permute-done.5), slice={[0:128], [0:1024]} | slice | bytes 524288 | tf_op jit(solution)/shard_map/slice | solution.py:108
  66.9 1.8 %copy.19 = bf16[128,8,128]{2,0,1:T(8,128)(2,1)} copy(bf16[128,8,128]{0,2,1:T(8,128)(2,1)} %bitcast.76) | data formatting | bytes 524288 | tf_op jit(solution)/shard_map/concatenate | solution.py:108
  68.7 2.1 %pad_maximum_fusion = bf16[384,8,128]{2,0,1:T(8,128)(2,1)} fusion(bf16[128,8,128]{2,0,1:T(8,128)(2,1)} %copy.19, bf16[128,8,128]{2,0,1:T(8,128)(2,1)} %copy.18, bf16[128,8,128]{2,0,1:T(8,128)(2,1)} %copy.17), kind=kLoop, calls=%fused_computation.22 | loop fusion | flops 2359296 | bytes 1572864 | tf_op jit(solution)/shard_map/concatenate | solution.py:108
  70.7 2.7 %gather_fusion.4 = bf16[8,384,128]{2,1,0:T(8,128)(2,1)} fusion(bf16[384,8,128]{2,0,1:T(8,128)(2,1)} %pad_maximum_fusion, s32[1024]{0:T(1024)S(1)} %pad_clamp_fusion), kind=kCustom, calls=%fused_computation.4 | custom fusion | bytes 1572896 | tf_op jit(solution)/shard_map/jit(_take)/gather | solution.py:76
  73.4 2.3 %copy.20 = bf16[384,8,128]{0,2,1:T(8,128)(2,1)} copy(bf16[384,8,128]{2,0,1:T(8,128)(2,1)} %bitcast.70) | data formatting | bytes 1572864 | tf_op jit(solution)/shard_map/jit(_take)/gather | solution.py:76
  80.9 1.7 %fusion.4 = f32[1024,256]{1,0:T(8,128)} fusion(bf16[1,1024,1024]{2,1,0:T(8,128)(2,1)S(1)} %copy-done, bf16[128,256]{1,0:T(8,128)(2,1)S(1)} %fusion.20, bf16[768,256]{1,0:T(8,128)(2,1)S(1)} %copy-done.2, bf16[128,256]{1,0:T(8,128)(2,1)S(1)} %fusion.21), kind=kOutput, calls=%fused_computation.10 | convolution fusion | flops 538443776 | bytes 3670016 | tf_op jit(solution)/shard_map/dot_general | solution.py:120
  82.6 2.4 %constant_dynamic-update-slice_fusion.13 = (bf16[1024,256]{1,0:T(8,128)(2,1)}, bf16[128,256]{1,0:T(8,128)(2,1)S(1)}) fusion(bf16[1024,128]{1,0:T(8,128)(2,1)S(1)} %bitcast_select_fusion.1, f32[1024,256]{1,0:T(8,128)} %fusion.4, f32[1024,256]{1,0:T(8,128)S(1)} %fusion.2, bf16[384,256]{1,0:T(8,128)(2,1)} %copy-done.8), kind=kOutput, calls=%fused_computation.65 | convolution fusion | flops 135036928 | bytes 2818048 | tf_op jit(solution)/shard_map/dot_general | solution.py:125
  85.0 2.5 %collective-permute-start.12 = (bf16[128,256]{1,0:T(8,128)(2,1)S(1)}, bf16[128,256]{1,0:T(8,128)(2,1)}, u32[]{:S(2)}, u32[]{:S(2)}) collective-permute-start(bf16[128,256]{1,0:T(8,128)(2,1)S(1)} %get-tuple-element.20), channel_id=1, source_target_pairs={{0,2},{2,4},{4,6},{6,8},{8,10},{10,12},{12,14},{14,0},{1,3},{3,5},... | collective-permute-start | bytes 196616 | tf_op jit(solution)/shard_map/ppermute | solution.py:59
  88.3 3.0 %collective-permute-start.15 = (bf16[128,256]{1,0:T(8,128)(2,1)S(1)}, bf16[128,256]{1,0:T(8,128)(2,1)}, u32[]{:S(2)}, u32[]{:S(2)}) collective-permute-start(bf16[128,256]{1,0:T(8,128)(2,1)S(1)} %get-tuple-element.20), channel_id=1, source_target_pairs={{0,8},{2,10},{4,12},{6,14},{8,0},{10,2},{12,4},{14,6},{1,9},{3,11}... | collective-permute-start | bytes 196616 | tf_op jit(solution)/shard_map/ppermute | solution.py:59
  92.2 1.7 %slice_select_fusion = bf16[128,8,128]{2,0,1:T(8,128)(2,1)} fusion(bf16[384,8,128]{2,0,1:T(8,128)(2,1)} %bitcast.71, pred[8]{0:T(512)(128)(4,1)S(1)} %copy-done.12), kind=kLoop, calls=%fused_computation.34 | loop fusion | flops 131072 | bytes 524296 | tf_op jit(solution)/shard_map/jit(_take)/select_n | solution.py:76
  93.9 1.8 %copy.22 = bf16[128,8,128]{0,2,1:T(8,128)(2,1)} copy(bf16[128,8,128]{2,0,1:T(8,128)(2,1)} %slice_select_fusion) | data formatting | bytes 524288 | tf_op jit(solution)/shard_map/slice | solution.py:131
  95.7 3.0 %collective-permute-start.17 = (bf16[128,256]{1,0:T(8,128)(2,1)S(1)}, bf16[128,256]{1,0:T(8,128)(2,1)S(1)}, u32[]{:S(2)}, u32[]{:S(2)}) collective-permute-start(bf16[128,256]{1,0:T(8,128)(2,1)S(1)} %get-tuple-element.20), channel_id=1, source_target_pairs={{0,12},{2,14},{4,0},{6,2},{8,4},{10,6},{12,8},{14,10},{1,13},{3,15... | collective-permute-start | bytes 196616 | tf_op jit(solution)/shard_map/ppermute | solution.py:59
  107.0 2.6 %fusion.10 = bf16[1,1024,256]{2,1,0:T(8,128)(2,1)} fusion(f32[1024,256]{1,0:T(8,128)S(1)} %copy-done.1, bf16[1024,128]{1,0:T(8,128)(2,1)S(1)} %bitcast_select_fusion.1, bf16[128,1024]{0,1:T(8,128)(2,1)} %bitcast.74, bf16[1024,256]{1,0:T(8,128)(2,1)} %constant_dynamic-update-slice_fusion.6), kind=kOutput, calls=%fused_computation.16 | convolution fusion | flops 134774784 | bytes 2621440 | tf_op jit(solution)/shard_map/dot_general | solution.py:133
  (94 shorter events, 38.0 us)
Async XLA Ops:
  0.0 1.8 %copy-start = (bf16[1,1024,1024]{2,1,0:T(8,128)(2,1)S(1)}, bf16[1,1024,1024]{2,1,0:T(8,128)(2,1)}, u32[]{:S(2)}) copy-start(bf16[1,1024,1024]{2,1,0:T(8,128)(2,1)} %param.8) | copy-start | bytes 6291460
  1.8 8.3 %copy-start.5 = (bf16[4,1,64,1,256]{4,2,3,1,0:T(8,128)(2,1)S(1)}, bf16[4,1,64,1,256]{4,2,3,1,0:T(8,128)(2,1)}, u32[]{:S(2)}) copy-start(bf16[4,1,64,1,256]{4,2,3,1,0:T(8,128)(2,1)} %param.13) | copy-start | bytes 393220
  3.6 13.5 %copy-start.9 = (s32[1,2,128]{2,1,0:T(2,128)S(1)}, s32[1,2,128]{2,1,0:T(2,128)}, u32[]{:S(2)}) copy-start(s32[1,2,128]{2,1,0:T(2,128)} %param.10) | copy-start | bytes 3076
  4.5 39.1 %collective-permute-start.6 = (bf16[128,256]{1,0:T(8,128)(2,1)}, bf16[128,256]{1,0:T(8,128)(2,1)}, u32[]{:S(2)}, u32[]{:S(2)}) collective-permute-start(bf16[128,256]{1,0:T(8,128)(2,1)} %get-tuple-element.18), channel_id=1, source_target_pairs={{0,4},{2,6},{4,8},{6,10},{8,12},{10,14},{12,0},{14,2},{1,5},{3,7},... | collective-permute-start | bytes 196616 | tf_op jit(solution)/shard_map/ppermute | solution.py:59
  7.6 40.5 %collective-permute-start.7 = (bf16[128,256]{1,0:T(8,128)(2,1)}, bf16[128,256]{1,0:T(8,128)(2,1)}, u32[]{:S(2)}, u32[]{:S(2)}) collective-permute-start(bf16[128,256]{1,0:T(8,128)(2,1)} %get-tuple-element.18), channel_id=1, source_target_pairs={{0,6},{2,8},{4,10},{6,12},{8,14},{10,0},{12,2},{14,4},{1,7},{3,9},... | collective-permute-start | bytes 196616 | tf_op jit(solution)/shard_map/ppermute | solution.py:59
  10.7 14.9 %collective-permute-start.2 = (bf16[1,1,64,1,256]{4,2,3,1,0:T(8,128)(2,1)}, bf16[1,1,64,1,256]{4,2,3,1,0:T(8,128)(2,1)}, u32[]{:S(2)}, u32[]{:S(2)}) collective-permute-start(bf16[1,1,64,1,256]{4,2,3,1,0:T(8,128)(2,1)} %get-tuple-element.10), channel_id=1, source_target_pairs={{0,8},{4,12},{8,0},{12,4},{1,9},{5,13},{9,1},{13,5},{2,10},{6,14},... | collective-permute-start | bytes 98312 | tf_op jit(solution)/shard_map/ppermute | solution.py:35
  12.0 14.6 %collective-permute-start.3 = (bf16[1,1,64,1,256]{4,2,3,1,0:T(8,128)(2,1)}, bf16[1,1,64,1,256]{4,2,3,1,0:T(8,128)(2,1)}, u32[]{:S(2)}, u32[]{:S(2)}) collective-permute-start(bf16[1,1,64,1,256]{4,2,3,1,0:T(8,128)(2,1)} %get-tuple-element.9), channel_id=1, source_target_pairs={{0,12},{4,0},{8,4},{12,8},{1,13},{5,1},{9,5},{13,9},{2,14},{6,2},{... | collective-permute-start | bytes 98312 | tf_op jit(solution)/shard_map/ppermute | solution.py:35
  14.7 13.3 %collective-permute-start.1 = (bf16[1,1,64,1,256]{4,2,3,1,0:T(8,128)(2,1)}, bf16[1,1,64,1,256]{4,2,3,1,0:T(8,128)(2,1)}, u32[]{:S(2)}, u32[]{:S(2)}) collective-permute-start(bf16[1,1,64,1,256]{4,2,3,1,0:T(8,128)(2,1)} %get-tuple-element.8), channel_id=1, source_target_pairs={{0,4},{4,8},{8,12},{12,0},{1,5},{5,9},{9,13},{13,1},{2,6},{6,10},{... | collective-permute-start | bytes 98312 | tf_op jit(solution)/shard_map/ppermute | solution.py:35
  15.3 2.4 %copy-start.11 = (pred[8]{0:T(512)(128)(4,1)}, pred[8]{0:T(512)(128)(4,1)S(1)}, u32[]{:S(2)}) copy-start(pred[8]{0:T(512)(128)(4,1)S(1)} %compare_and_fusion) | copy-start | bytes 28
  25.6 25.3 %collective-permute-start.8 = (bf16[128,256]{1,0:T(8,128)(2,1)}, bf16[128,256]{1,0:T(8,128)(2,1)}, u32[]{:S(2)}, u32[]{:S(2)}) collective-permute-start(bf16[128,256]{1,0:T(8,128)(2,1)} %get-tuple-element.18), channel_id=1, source_target_pairs={{0,8},{2,10},{4,12},{6,14},{8,0},{10,2},{12,4},{14,6},{1,9},{3,11}... | collective-permute-start | bytes 196616 | tf_op jit(solution)/shard_map/ppermute | solution.py:59
  26.6 27.0 %collective-permute-start.9 = (bf16[128,256]{1,0:T(8,128)(2,1)}, bf16[128,256]{1,0:T(8,128)(2,1)}, u32[]{:S(2)}, u32[]{:S(2)}) collective-permute-start(bf16[128,256]{1,0:T(8,128)(2,1)} %get-tuple-element.18), channel_id=1, source_target_pairs={{0,10},{2,12},{4,14},{6,0},{8,2},{10,4},{12,6},{14,8},{1,11},{3,13... | collective-permute-start | bytes 196616 | tf_op jit(solution)/shard_map/ppermute | solution.py:59
  27.9 13.4 %collective-permute-start = (bf16[256,256]{1,0:T(8,128)(2,1)}, bf16[256,256]{1,0:T(8,128)(2,1)}, u32[]{:S(2)}, u32[]{:S(2)}) collective-permute-start(bf16[256,256]{1,0:T(8,128)(2,1)} %get-tuple-element.12), channel_id=1, source_target_pairs={{0,2},{2,4},{4,6},{6,8},{8,10},{10,12},{12,14},{14,0},{1,3},{3,5},... | collective-permute-start | bytes 393224 | tf_op jit(solution)/shard_map/ppermute | solution.py:59
  36.0 7.7 %copy-start.4 = (bf16[256,256]{1,0:T(8,128)(2,1)S(1)}, bf16[256,256]{1,0:T(8,128)(2,1)}, u32[]{:S(2)}) copy-start(bf16[256,256]{1,0:T(8,128)(2,1)} %get-tuple-element.11) | copy-start | bytes 393220
  41.4 13.7 %collective-permute-start.10 = (bf16[128,256]{1,0:T(8,128)(2,1)}, bf16[128,256]{1,0:T(8,128)(2,1)S(1)}, u32[]{:S(2)}, u32[]{:S(2)}) collective-permute-start(bf16[128,256]{1,0:T(8,128)(2,1)} %get-tuple-element.18), channel_id=1, source_target_pairs={{0,12},{2,14},{4,0},{6,2},{8,4},{10,6},{12,8},{14,10},{1,13},{3,15... | collective-permute-start | bytes 196616 | tf_op jit(solution)/shard_map/ppermute | solution.py:59
  43.7 12.1 %collective-permute-start.11 = (bf16[256,256]{1,0:T(8,128)(2,1)S(1)}, bf16[256,256]{1,0:T(8,128)(2,1)S(1)}, u32[]{:S(2)}, u32[]{:S(2)}) collective-permute-start(bf16[256,256]{1,0:T(8,128)(2,1)S(1)} %copy-done.4), channel_id=1, source_target_pairs={{0,14},{2,0},{4,2},{6,4},{8,6},{10,8},{12,10},{14,12},{1,15},{3,1}... | collective-permute-start | bytes 393224 | tf_op jit(solution)/shard_map/ppermute | solution.py:59
  48.1 13.9 %collective-permute-start.4 = (bf16[128,1152]{0,1:T(8,128)(2,1)S(1)}, bf16[128,1152]{0,1:T(8,128)(2,1)S(1)}, u32[]{:S(2)}, u32[]{:S(2)}) collective-permute-start(bf16[128,1152]{0,1:T(8,128)(2,1)S(1)} %get-tuple-element.5), channel_id=1, source_target_pairs={{0,2},{2,4},{4,6},{6,8},{8,10},{10,12},{12,14},{1,3},{3,5},{5,7},{... | collective-permute-start | bytes 884744 | tf_op jit(solution)/shard_map/ppermute | solution.py:25
  50.9 14.3 %collective-permute-start.5 = (bf16[128,1152]{0,1:T(8,128)(2,1)}, bf16[128,1152]{0,1:T(8,128)(2,1)}, u32[]{:S(2)}, u32[]{:S(2)}) collective-permute-start(bf16[128,1152]{0,1:T(8,128)(2,1)} %get-tuple-element.6), channel_id=1, source_target_pairs={{2,0},{4,2},{6,4},{8,6},{10,8},{12,10},{14,12},{3,1},{5,3},{7,5},{... | collective-permute-start | bytes 884744 | tf_op jit(solution)/shard_map/ppermute | solution.py:25
  55.7 7.7 %copy-start.6 = (bf16[256,256]{1,0:T(8,128)(2,1)}, bf16[256,256]{1,0:T(8,128)(2,1)S(1)}, u32[]{:S(2)}) copy-start(bf16[256,256]{1,0:T(8,128)(2,1)S(1)} %collective-permute-done.11) | copy-start | bytes 393220
  68.7 7.0 %copy-start.10 = (pred[1024]{0:T(1024)(128)(4,1)S(1)}, pred[1024]{0:T(1024)(128)(4,1)}, u32[]{:S(2)}) copy-start(pred[1024]{0:T(1024)(128)(4,1)} %broadcast_bitcast_fusion) | copy-start | bytes 3076
  75.7 2.9 %copy-start.14 = (f32[128]{0:T(128)S(1)}, f32[128]{0:T(128)}, u32[]{:S(2)}) copy-start(f32[128]{0:T(128)} %get-tuple-element.13) | copy-start | bytes 1540
  75.7 4.1 %copy-start.7 = (bf16[256,256]{1,0:T(8,128)(2,1)S(1)}, bf16[256,256]{1,0:T(8,128)(2,1)}, u32[]{:S(2)}) copy-start(bf16[256,256]{1,0:T(8,128)(2,1)} %copy-done.6) | copy-start | bytes 393220
  75.7 4.1 %copy-start.13 = (f32[128]{0:T(128)S(1)}, f32[128]{0:T(128)}, u32[]{:S(2)}) copy-start(f32[128]{0:T(128)} %get-tuple-element.14) | copy-start | bytes 1540
  75.7 5.2 %copy-start.2 = (bf16[768,256]{1,0:T(8,128)(2,1)S(1)}, bf16[768,256]{1,0:T(8,128)(2,1)}, u32[]{:S(2)}) copy-start(bf16[768,256]{1,0:T(8,128)(2,1)} %slice_bitcast_fusion) | copy-start | bytes 1179652
  82.6 9.6 %copy-start.12 = (pred[8]{0:T(512)(128)(4,1)S(1)}, pred[8]{0:T(512)(128)(4,1)}, u32[]{:S(2)}) copy-start(pred[8]{0:T(512)(128)(4,1)} %copy-done.11) | copy-start | bytes 28
  85.0 22.0 %copy-start.1 = (f32[1024,256]{1,0:T(8,128)S(1)}, f32[1024,256]{1,0:T(8,128)}, u32[]{:S(2)}) copy-start(f32[1024,256]{1,0:T(8,128)} %fusion.4) | copy-start | bytes 3145732
  85.0 10.7 %collective-permute-start.12 = (bf16[128,256]{1,0:T(8,128)(2,1)S(1)}, bf16[128,256]{1,0:T(8,128)(2,1)}, u32[]{:S(2)}, u32[]{:S(2)}) collective-permute-start(bf16[128,256]{1,0:T(8,128)(2,1)S(1)} %get-tuple-element.20), channel_id=1, source_target_pairs={{0,2},{2,4},{4,6},{6,8},{8,10},{10,12},{12,14},{14,0},{1,3},{3,5},... | collective-permute-start | bytes 196616 | tf_op jit(solution)/shard_map/ppermute | solution.py:59
  87.5 12.7 %collective-permute-start.13 = (bf16[128,256]{1,0:T(8,128)(2,1)S(1)}, bf16[128,256]{1,0:T(8,128)(2,1)}, u32[]{:S(2)}, u32[]{:S(2)}) collective-permute-start(bf16[128,256]{1,0:T(8,128)(2,1)S(1)} %get-tuple-element.20), channel_id=1, source_target_pairs={{0,4},{2,6},{4,8},{6,10},{8,12},{10,14},{12,0},{14,2},{1,5},{3,7},... | collective-permute-start | bytes 196616 | tf_op jit(solution)/shard_map/ppermute | solution.py:59
  88.1 14.1 %collective-permute-start.14 = (bf16[128,256]{1,0:T(8,128)(2,1)S(1)}, bf16[128,256]{1,0:T(8,128)(2,1)}, u32[]{:S(2)}, u32[]{:S(2)}) collective-permute-start(bf16[128,256]{1,0:T(8,128)(2,1)S(1)} %get-tuple-element.20), channel_id=1, source_target_pairs={{0,6},{2,8},{4,10},{6,12},{8,14},{10,0},{12,2},{14,4},{1,7},{3,9},... | collective-permute-start | bytes 196616 | tf_op jit(solution)/shard_map/ppermute | solution.py:59
  88.3 15.3 %collective-permute-start.15 = (bf16[128,256]{1,0:T(8,128)(2,1)S(1)}, bf16[128,256]{1,0:T(8,128)(2,1)}, u32[]{:S(2)}, u32[]{:S(2)}) collective-permute-start(bf16[128,256]{1,0:T(8,128)(2,1)S(1)} %get-tuple-element.20), channel_id=1, source_target_pairs={{0,8},{2,10},{4,12},{6,14},{8,0},{10,2},{12,4},{14,6},{1,9},{3,11}... | collective-permute-start | bytes 196616 | tf_op jit(solution)/shard_map/ppermute | solution.py:59
  91.3 13.9 %collective-permute-start.16 = (bf16[128,256]{1,0:T(8,128)(2,1)S(1)}, bf16[128,256]{1,0:T(8,128)(2,1)S(1)}, u32[]{:S(2)}, u32[]{:S(2)}) collective-permute-start(bf16[128,256]{1,0:T(8,128)(2,1)S(1)} %get-tuple-element.20), channel_id=1, source_target_pairs={{0,10},{2,12},{4,14},{6,0},{8,2},{10,4},{12,6},{14,8},{1,11},{3,13... | collective-permute-start | bytes 196616 | tf_op jit(solution)/shard_map/ppermute | solution.py:59
  95.7 10.1 %collective-permute-start.17 = (bf16[128,256]{1,0:T(8,128)(2,1)S(1)}, bf16[128,256]{1,0:T(8,128)(2,1)S(1)}, u32[]{:S(2)}, u32[]{:S(2)}) collective-permute-start(bf16[128,256]{1,0:T(8,128)(2,1)S(1)} %get-tuple-element.20), channel_id=1, source_target_pairs={{0,12},{2,14},{4,0},{6,2},{8,4},{10,6},{12,8},{14,10},{1,13},{3,15... | collective-permute-start | bytes 196616 | tf_op jit(solution)/shard_map/ppermute | solution.py:59
  100.1 6.3 %collective-permute-start.18 = (bf16[128,256]{1,0:T(8,128)(2,1)S(1)}, bf16[128,256]{1,0:T(8,128)(2,1)S(1)}, u32[]{:S(2)}, u32[]{:S(2)}) collective-permute-start(bf16[128,256]{1,0:T(8,128)(2,1)S(1)} %get-tuple-element.20), channel_id=1, source_target_pairs={{0,14},{2,0},{4,2},{6,4},{8,6},{10,8},{12,10},{14,12},{1,15},{3,1}... | collective-permute-start | bytes 196616 | tf_op jit(solution)/shard_map/ppermute | solution.py:59
  (2 other events, 1.9 us)
